TPU v7x, 32 devices: a whole 2x2x4 slice. The times are simulated.
32 devices in a mesh: rep: 8 (over z, x), tile: 4 (over y, core).
Axes of the slice: x: 2, y: 2, z: 4, core: 2. Of those that a mesh axis runs over, the one named last changes fastest.
Arguments:
- features: bfloat16 [16, 48, 72, 1536], P('rep', 'tile'), may hold values from -6 to 6
- conv_out: bfloat16 [16, 48, 72, 256], P('rep', 'tile'), may hold values from -6 to 6
- conv_weight: bfloat16 [9, 1536, 256], replicated, may hold values from -0.0546875 to 0.0546875
- norm_gain_vector: float32 [256], replicated, may hold values from 0.5 to 1.5
- norm_shift_vector: float32 [256], replicated, may hold values from -3 to 3
- class_map: float32 [3, 256], replicated, may hold values from -3 to 3
- labels: int32 [16, 48, 72], P('rep', 'tile'), may hold values from 0 to 2
- class_weight: int32 [3], replicated, may hold values from 1 to 39
Outputs:
- grad_features: bfloat16 [16, 48, 72, 1536], P('rep', 'tile')
- grad_weight: float32 [1536, 9, 256], P(('rep', 'tile'))
- grad_gain: float32 [256], replicated
- grad_shift: float32 [256], replicated
- grad_class: float32 [3, 256], replicated
- loss: float32 [], replicated
All inputs are finite; a program needn't handle non-finite values.
Results may differ from a plain program's by a relative error of at most 0.0049.
Values may be sent and summed in bfloat16 or wider, within the bound.
No kernel may reach another device: no remote copies, remote signals or barrier semaphores. Data moves between devices by JAX's collectives and lax.ppermute only.
A program may use at most 256 MiB of HBM per device.

v0:
```python
import jax
import jax.numpy as jnp
from jax import lax
from jax.sharding import PartitionSpec as P

IMG_DEV = 2
H = 48
W = 72
RATE = 12


def padded(x, sides, width):
    for axis, dim in sides:
        size, length = (lax.axis_size(axis), x.shape[dim])
        up = [(i, (i + 1) % size) for i in range(size - 1)]
        down = [(j, i) for i, j in up]
        last = lax.slice_in_dim(x, length - width, length, axis=dim)
        first = lax.slice_in_dim(x, 0, width, axis=dim)
        before = lax.ppermute(last, axis, up)
        after = lax.ppermute(first, axis, down)
        x = jnp.concatenate([before, x, after], axis=dim)
    return x


def body(
    features,
    conv_out,
    conv_weight,
    norm_gain_vector,
    norm_shift_vector,
    class_map,
    labels,
    class_weight,
):
    highest = lax.Precision.HIGHEST
    images, tile_rows, columns, in_chans = features.shape
    out_chans = conv_out.shape[3]
    local_pix = images * tile_rows * columns
    per_replica_part = IMG_DEV * H * W
    all_pix = lax.axis_size("rep") * per_replica_part
    yvals = conv_out.astype(jnp.float32).reshape(local_pix, out_chans)
    column_sum = lax.psum(jnp.sum(yvals, 0), "tile")
    centre_offset = yvals - column_sum / per_replica_part
    variance = lax.psum(jnp.sum(centre_offset * centre_offset, 0), "tile") / per_replica_part
    inverse_deviation = lax.rsqrt(variance + 1e-05)
    normalized_input = centre_offset * inverse_deviation
    preactivation_values = norm_gain_vector * normalized_input + norm_shift_vector
    zvals = jnp.maximum(preactivation_values, 0.0)
    logits = jnp.dot(zvals, class_map.T, precision=highest)
    onehot = (
        labels.reshape(local_pix, 1) == jnp.arange(class_map.shape[0], dtype=jnp.int32)
    ).astype(jnp.float32)
    weights_pix = jnp.sum(onehot * class_weight.astype(jnp.float32), -1)
    top_val = jnp.max(logits, -1, keepdims=True)
    log_total = top_val[:, 0] + jnp.log(jnp.sum(jnp.exp(logits - top_val), -1))
    cross = log_total - jnp.sum(onehot * logits, -1)
    weight_total, loss_total = lax.psum(
        (jnp.sum(weights_pix), jnp.sum(weights_pix * cross)), ("rep", "tile")
    )
    mean_weight = weight_total / all_pix
    loss = loss_total / mean_weight / all_pix
    probs = jnp.exp(logits - log_total[:, None])
    grad_logit = (weights_pix / mean_weight)[:, None] * (probs - onehot)
    class_local_slice = jnp.dot(grad_logit.T, zvals, precision=highest)
    grad_z = jnp.dot(grad_logit, class_map, precision=highest)
    preactivation_gradient = jnp.where(preactivation_values > 0, grad_z, 0.0)
    first_gradient_sum, second_gradient_sum, class_tile = lax.psum(
        (
            jnp.sum(preactivation_gradient, 0),
            jnp.sum(preactivation_gradient * normalized_input, 0),
            class_local_slice,
        ),
        "tile",
    )
    grad_shift, grad_gain, grad_class = lax.psum(
        (first_gradient_sum, second_gradient_sum, class_tile), "rep"
    )
    normalized_output_gradient = (
        norm_gain_vector
        * inverse_deviation
        * (
            preactivation_gradient
            - first_gradient_sum / per_replica_part
            - normalized_input * second_gradient_sum / per_replica_part
        )
    ).astype(jnp.bfloat16)
    normalized_output_gradient = normalized_output_gradient.reshape(
        images, tile_rows, columns, out_chans
    )
    extended = padded(normalized_output_gradient, (("tile", 1),), RATE)
    extended = jnp.pad(extended, ((0, 0), (0, 0), (RATE, RATE), (0, 0)))
    shifted_list = []
    for tap_index in range(9):
        row_off = RATE - (tap_index // 3 - 1) * RATE
        col_off = RATE - (tap_index % 3 - 1) * RATE
        piece = extended[:, row_off : row_off + tile_rows, col_off : col_off + columns, :]
        shifted_list.append(piece.reshape(local_pix, out_chans))
    accum_grad = jnp.zeros((local_pix, in_chans), jnp.float32)
    for tap_index in range(9):
        accum_grad = accum_grad + lax.dot_general(
            shifted_list[tap_index],
            conv_weight[tap_index],
            (((1,), (1,)), ((), ())),
            preferred_element_type=jnp.float32,
        )
    grad_features = accum_grad.astype(jnp.bfloat16).reshape(images, tile_rows, columns, in_chans)
    flat_x = features.reshape(local_pix, in_chans)
    parts_list = [
        lax.dot_general(
            flat_x, shifted, (((0,), (0,)), ((), ())), preferred_element_type=jnp.float32
        )
        for shifted in shifted_list
    ]
    grad_weight = lax.psum_scatter(
        jnp.stack(parts_list, 1), ("rep", "tile"), scatter_dimension=0, tiled=True
    )
    return (grad_features, grad_weight, grad_gain, grad_shift, grad_class, loss)


def solution(mesh):
    in_specs = (
        P("rep", "tile", None, None),
        P("rep", "tile", None, None),
        P(),
        P(),
        P(),
        P(),
        P("rep", "tile", None),
        P(),
    )
    out_specs = (P("rep", "tile", None, None), P(("rep", "tile"), None, None), P(), P(), P(), P())
    return jax.shard_map(body, mesh=mesh, in_specs=in_specs, out_specs=out_specs, check_vma=False)
```

profile of v0, /device:TPU:0, one launch (start us, length us, event | category | flops | bytes accessed | tf_op | source)
XLA Modules:
  0.0 405.0 jit_solution(10787423601491690530)
XLA Ops:
  8.7 8.4 %psum.70 = f32[256]{0:T(256)S(1)} all-reduce(f32[256]{0:T(256)S(1)} %convert_reduce_fusion), channel_id=1, replica_groups=mesh['rep'=8,'tile'=4] {'tile'}, use_global_device_ids=true, to_apply=%region_1.0 | all-reduce | flops 256 | bytes 2048 | tf_op jit(solution)/shard_map/psum | solution.py:42
  18.5 5.8 %psum.71 = f32[256]{0:T(256)S(1)} all-reduce(f32[256]{0:T(256)S(1)} %multiply_reduce_fusion.1), channel_id=1, replica_groups=mesh['rep'=8,'tile'=4] {'tile'}, use_global_device_ids=true, to_apply=%region_3.0 | all-reduce | flops 256 | bytes 2048 | tf_op jit(solution)/shard_map/psum | solution.py:44
  27.7 2.5 fusion.63
  31.5 39.9 %all-reduce.1 = (f32[]{:T(128)}, f32[]{:T(128)}) all-reduce(f32[]{:T(128)} %get-tuple-element.31, f32[]{:T(128)} %get-tuple-element.40), channel_id=1, replica_groups=mesh['rep'=8,'tile'=4] {'rep','tile'}, use_global_device_ids=true, to_apply=%region_6.0 | all-reduce | flops 2 | bytes 16 | tf_op jit(solution)/shard_map/psum | solution.py:57
  73.1 4.6 %fusion.61 = (f32[256]{0:T(256)S(1)}, f32[256]{0:T(256)S(1)}, f32[1728,256]{1,0:T(8,128)}) fusion(f32[256]{0:T(256)S(1)} %get-tuple-element.49, f32[256]{0:T(256)S(1)} %broadcast_multiply_fusion.1, bf16[2,12,72,256]{3,2,1,0:T(8,128)(2,1)} %param.9, f32[3,256]{1,0:T(4,128)S(1)} %copy-done, f32[1728,3]{0,1:T(4,128)S(1)} %get-tuple-element.51, ...), kind=kOutput, calls=%fused_computation.92 | convolution fusion | flops 20374336 | bytes 4474368 | tf_op jit(solution)/shard_map/dot_general | solution.py:65
  77.6 6.9 %all-reduce.3 = (f32[256]{0:T(256)S(1)}, f32[256]{0:T(256)S(1)}, f32[3,256]{1,0:T(4,128)S(1)}) all-reduce(f32[256]{0:T(256)S(1)} %get-tuple-element.25, f32[256]{0:T(256)S(1)} %get-tuple-element.24, f32[3,256]{1,0:T(4,128)S(1)} %fusion.16), channel_id=1, replica_groups=mesh['rep'=8,'tile'=4] {'tile'}, use_global_device_ids=true, to_apply=%region_12.13 | all-reduce | flops 1280 | bytes 10240 | tf_op jit(solution)/shard_map/psum | solution.py:67
  84.5 2.3 multiply_convert_fusion
  86.9 1.5 collective-permute-start
  90.4 3.8 collective-permute-done.1
  94.2 1.8 fusion.5
  96.1 2.8 fusion.14
  98.9 2.8 fusion.13
  101.7 2.8 fusion.12
  104.4 2.8 fusion.11
  107.2 2.8 fusion.10
  110.0 2.8 fusion.9
  112.7 2.7 fusion.8
  115.5 2.8 fusion.7
  118.3 2.8 fusion.6
  121.0 19.0 %copy.18 = f32[1536,9,256]{2,1,0:T(8,128)} copy(f32[1536,9,256]{0,2,1:T(8,128)} %fusion.6) | data formatting | bytes 28311552 | tf_op jit(solution)/shard_map/stack | solution.py:115
  140.7 21.3 %all-reduce.2 = (f32[256]{0:T(256)}, f32[256]{0:T(256)}, f32[3,256]{1,0:T(4,128)}) all-reduce(f32[256]{0:T(256)S(1)} %get-tuple-element.37, f32[256]{0:T(256)S(1)} %get-tuple-element.38, f32[3,256]{1,0:T(4,128)S(1)} %get-tuple-element.39), channel_id=1, replica_groups=mesh['rep'=8,'tile'=4] {'rep'}, use_global_device_ids=true, to_apply=%region_14.15 | all-reduce | flops 1280 | bytes 10240 | tf_op jit(solution)/shard_map/psum | solution.py:75
  162.0 7.7 %fusion.33 = f32[1728,1536]{1,0:T(8,128)} fusion(bf16[1728,256]{1,0:T(8,128)(2,1)S(1)} %multiply_convert_fusion, bf16[9,1536,256]{2,1,0:T(8,128)(2,1)} %param.10), kind=kOutput, calls=%fused_computation.52 | convolution fusion | flops 1358954496 | bytes 12288000 | tf_op jit(solution)/shard_map/dot_general | solution.py:100
  170.3 8.2 %fusion.26 = f32[1728,1536]{1,0:T(8,128)} fusion(bf16[1728,256]{1,0:T(8,128)(2,1)S(1)} %bitcast.174, bf16[9,1536,256]{2,1,0:T(8,128)(2,1)} %param.10), kind=kOutput, calls=%fused_computation.45 | convolution fusion | flops 1358954496 | bytes 12288000 | tf_op jit(solution)/shard_map/dot_general | solution.py:100
  178.5 6.4 %fusion.29 = f32[1728,1536]{1,0:T(8,128)} fusion(bf16[1728,256]{1,0:T(8,128)(2,1)S(1)} %bitcast.173, bf16[9,1536,256]{2,1,0:T(8,128)(2,1)S(1)} %bitcast.167), kind=kOutput, calls=%fused_computation.48 | convolution fusion | flops 1358954496 | bytes 12288000 | tf_op jit(solution)/shard_map/dot_general | solution.py:100
  184.9 6.3 %fusion.31 = f32[1728,1536]{1,0:T(8,128)} fusion(bf16[1728,256]{1,0:T(8,128)(2,1)S(1)} %bitcast.172, bf16[9,1536,256]{2,1,0:T(8,128)(2,1)S(1)} %bitcast.167), kind=kOutput, calls=%fused_computation.50 | convolution fusion | flops 1358954496 | bytes 12288000 | tf_op jit(solution)/shard_map/dot_general | solution.py:100
  191.2 6.3 %fusion.35 = f32[1728,1536]{1,0:T(8,128)} fusion(bf16[1728,256]{1,0:T(8,128)(2,1)S(1)} %bitcast.171, bf16[9,1536,256]{2,1,0:T(8,128)(2,1)S(1)} %bitcast.167), kind=kOutput, calls=%fused_computation.54 | convolution fusion | flops 1358954496 | bytes 12288000 | tf_op jit(solution)/shard_map/dot_general | solution.py:100
  197.6 5.7 %fusion.37 = f32[1728,1536]{1,0:T(8,128)} fusion(bf16[1728,256]{1,0:T(8,128)(2,1)S(1)} %bitcast.170, bf16[9,1536,256]{2,1,0:T(8,128)(2,1)S(1)} %bitcast.167), kind=kOutput, calls=%fused_computation.56 | convolution fusion | flops 1358954496 | bytes 12288000 | tf_op jit(solution)/shard_map/dot_general | solution.py:100
  203.3 5.6 %fusion.41 = f32[1728,1536]{1,0:T(8,128)} fusion(bf16[1728,256]{1,0:T(8,128)(2,1)S(1)} %bitcast.169, bf16[9,1536,256]{2,1,0:T(8,128)(2,1)S(1)} %bitcast.167), kind=kOutput, calls=%fused_computation.60 | convolution fusion | flops 1358954496 | bytes 12288000 | tf_op jit(solution)/shard_map/dot_general | solution.py:100
  209.0 6.2 %fusion.39 = f32[1728,1536]{1,0:T(8,128)} fusion(bf16[1728,256]{1,0:T(8,128)(2,1)S(1)} %bitcast.164, bf16[9,1536,256]{2,1,0:T(8,128)(2,1)S(1)} %bitcast.167), kind=kOutput, calls=%fused_computation.58 | convolution fusion | flops 1358954496 | bytes 12288000 | tf_op jit(solution)/shard_map/dot_general | solution.py:100
  215.1 30.1 %add_convert_fusion = bf16[1728,1536]{1,0:T(8,128)(2,1)} fusion(f32[1728,1536]{1,0:T(8,128)} %fusion.26, f32[1728,1536]{1,0:T(8,128)} %fusion.29, f32[1728,1536]{1,0:T(8,128)} %fusion.31, f32[1728,1536]{1,0:T(8,128)} %fusion.33, f32[1728,1536]{1,0:T(8,128)} %fusion.35, f32[1728,1536]{1,0:T(8,128)} %fusion.37, f32[1728,1536]{1,0:T(8,128)} %fusion.41, ...), kind=kOutput, calls=%fused_computation.2 | convolution fusion | flops 1382842368 | bytes 91914240 | tf_op jit(solution)/shard_map/dot_general | solution.py:100
  245.2 149.6 %reduce-scatter.2.cloned.1.call-done = f32[48,9,256]{2,1,0:T(8,128)} async-done(((f32[1536,9,256]{2,1,0:T(8,128)}), f32[48,9,256]{2,1,0:T(8,128)}) %reduce-scatter.2.cloned.1.call-update) | async-done | bytes 442384 | tf_op jit(solution)/shard_map/reduce_scatter | solution.py:114
  394.8 2.2 copy.19
  (44 shorter events, 11.4 us)
Async XLA Ops:
  7.2 20.6 %copy-start = (f32[3,256]{1,0:T(4,128)S(1)}, f32[3,256]{1,0:T(4,128)}, u32[]{:S(2)}) copy-start(f32[3,256]{1,0:T(4,128)} %param.13) | copy-start | bytes 9220
  7.2 64.9 %copy-start.6 = (f32[256]{0:T(256)S(1)}, f32[256]{0:T(256)}, u32[]{:S(2)}) copy-start(f32[256]{0:T(256)} %param.11) | copy-start | bytes 3076
  7.2 64.9 %copy-start.7 = (f32[256]{0:T(256)S(1)}, f32[256]{0:T(256)}, u32[]{:S(2)}) copy-start(f32[256]{0:T(256)} %param.12) | copy-start | bytes 3076
  7.2 387.6 %reduce-scatter.2.cloned.1.call-start = ((), (), s32[]{:S(2)}) async-start(), calls=%async_computation.1 | async-start | bytes 25952256 | tf_op jit(solution)/shard_map/reduce_scatter | solution.py:114
  73.1 23.0 %slice-start = ((s8[5308416]{0:T(1024)(128)(4,1)}), s8[1114112]{0:T(1024)(128)(4,1)S(1)}, s32[]{:S(2)}) async-start(s8[5308416]{0:T(1024)(128)(4,1)} %bitcast.158), calls=%async_computation.2 | async-start | bytes 2228224
  84.5 11.5 %slice-start.1 = ((s8[5308416]{0:T(1024)(128)(4,1)}), s8[4194304]{0:T(1024)(128)(4,1)S(1)}, s32[]{:S(2)}) async-start(s8[5308416]{0:T(1024)(128)(4,1)} %bitcast.158), calls=%async_computation.3 | async-start | bytes 8388608
  86.9 3.5 collective-permute-start
  88.4 5.8 %collective-permute-start.1 = (bf16[2,12,72,256]{3,2,1,0:T(8,128)(2,1)S(1)}, bf16[2,12,72,256]{3,2,1,0:T(8,128)(2,1)S(1)}, u32[]{:S(2)}, u32[]{:S(2)}) collective-permute-start(bf16[2,12,72,256]{3,2,1,0:T(8,128)(2,1)S(1)} %bitcast.161), channel_id=1, source_target_pairs={{1,0},{2,1},{3,2},{5,4},{6,5},{7,6},{9,8},{10,9},{11,10},{13,12},{... | collective-permute-start | bytes 2654216 | tf_op jit(solution)/shard_map/ppermute | solution.py:20
  90.4 25.1 %copy-start.4 = (bf16[2,12,72,256]{3,2,1,0:T(8,128)(2,1)}, bf16[2,12,72,256]{3,2,1,0:T(8,128)(2,1)S(1)}, u32[]{:S(2)}) copy-start(bf16[2,12,72,256]{3,2,1,0:T(8,128)(2,1)S(1)} %collective-permute-done) | copy-start | bytes 2654212
  96.0 22.2 %copy-start.2 = (bf16[2,36,96,256]{3,2,1,0:T(8,128)(2,1)}, bf16[2,36,96,256]{3,2,1,0:T(8,128)(2,1)S(1)}, u32[]{:S(2)}) copy-start(bf16[2,36,96,256]{3,2,1,0:T(8,128)(2,1)S(1)} %fusion.5) | copy-start | bytes 10616836
  162.0 7.7 %copy-start.3 = (bf16[2,36,96,256]{3,2,1,0:T(8,128)(2,1)S(1)}, bf16[2,36,96,256]{3,2,1,0:T(8,128)(2,1)}, u32[]{:S(2)}) copy-start(bf16[2,36,96,256]{3,2,1,0:T(8,128)(2,1)} %copy-done.2) | copy-start | bytes 10616836
  169.7 8.8 %slice-start.2 = ((s8[7077888]{0:T(1024)(128)(4,1)}), s8[2883584]{0:T(1024)(128)(4,1)S(1)}, s32[]{:S(2)}) async-start(s8[7077888]{0:T(1024)(128)(4,1)} %bitcast.166), calls=%async_computation.4 | async-start | bytes 5767168
  170.3 8.2 %slice-start.3 = ((s8[7077888]{0:T(1024)(128)(4,1)}), s8[4194304]{0:T(1024)(128)(4,1)S(1)}, s32[]{:S(2)}) async-start(s8[7077888]{0:T(1024)(128)(4,1)} %bitcast.166), calls=%async_computation.5 | async-start | bytes 8388608
  208.9 6.2 %copy-start.5 = (bf16[2,12,72,256]{3,2,1,0:T(8,128)(2,1)S(1)}, bf16[2,12,72,256]{3,2,1,0:T(8,128)(2,1)}, u32[]{:S(2)}) copy-start(bf16[2,12,72,256]{3,2,1,0:T(8,128)(2,1)} %copy-done.4) | copy-start | bytes 2654212
  215.1 181.9 %copy-start.1 = (f32[3,256]{1,0:T(4,128)S(1)}, f32[3,256]{1,0:T(4,128)}, u32[]{:S(2)}) copy-start(f32[3,256]{1,0:T(4,128)} %param.13) | copy-start | bytes 9220
Sparse Core Ops, SparseCore 0:
  140.1 254.6 reduce-scatter.1
where the time goes:
time: 406 us; the launch traced here: 405 us
  waiting for transfers between devices  154 us (38%)
  matrix products  116 us (29%)
  blocking collectives  82.2 us (20%)
  local copies, waits for them, and re-layouts  22.6 us (6%)
  between operations  16.6 us (4%)
  other arithmetic  11.1 us (3%)
    reduce_scatter x1, waiting for transfers between devices, body(): lax.psum_scatter(jnp.stack(parts_list, 1), ('rep', 'tile'), scatter_dimen...  150 us
    dot_general x9, matrix products, body(): lax.dot_general(shifted_list[tap_index], conv_weight[tap_index], (((1,),...  82.6 us
    psum x1, blocking collectives, body(): lax.psum((jnp.sum(weights_pix), jnp.sum(weights_pix * cross)), ('rep', 't...  39.9 us
    dot_general x9, matrix products, body(): lax.dot_general(flat_x, shifted, (((0,), (0,)), ((), ())), preferred_elem...  25 us
    psum x1, blocking collectives, body(): lax.psum((first_gradient_sum, second_gradient_sum, class_tile), 'rep')  21.3 us
    another operation x1, local copies, waits for them, and re-layouts, body(): jnp.stack(parts_list, 1)  19 us
    psum x1, blocking collectives, body(): column_sum = lax.psum(jnp.sum(yvals, 0), 'tile')  8.36 us
  transfers between devices with their start and end apart: 3, of which 3 were waited for; matrix products, arithmetic and copies ran while one was open for 21% of the time, Pallas kernels for 0%

commit v1 on v0

--- a/solution.py
+++ b/solution.py
@@ -55,7 +55,7 @@
     log_total = top_val[:, 0] + jnp.log(jnp.sum(jnp.exp(logits - top_val), -1))
     cross = log_total - jnp.sum(onehot * logits, -1)
     weight_total, loss_total = lax.psum(
-        (jnp.sum(weights_pix), jnp.sum(weights_pix * cross)), ("rep", "tile")
+        lax.psum((jnp.sum(weights_pix), jnp.sum(weights_pix * cross)), "tile"), "rep"
     )
     mean_weight = weight_total / all_pix
     loss = loss_total / mean_weight / all_pix

time: 406 us -> 391 us (0.963)
  blocking collectives: 82.2 us -> 67.5 us
    psum x1 -> x2, blocking collectives: 39.9 us -> 28.7 us  [the longest x1 22.4 us: body(): lax.psum(lax.psum((jnp.sum(weights_pix), jnp.sum(weights_pix * cross)), '...]
where the time goes in v1:
time: 391 us; the launch traced here: 390 us
  waiting for transfers between devices  153 us (39%)
  matrix products  116 us (30%)
  blocking collectives  67.5 us (17%)
  local copies, waits for them, and re-layouts  22.6 us (6%)
  between operations  16.6 us (4%)
  other arithmetic  11.1 us (3%)
    reduce_scatter x1, waiting for transfers between devices, body(): lax.psum_scatter(jnp.stack(parts_list, 1), ('rep', 'tile'), scatter_dimen...  150 us
    dot_general x9, matrix products, body(): lax.dot_general(shifted_list[tap_index], conv_weight[tap_index], (((1,),...  82.6 us
    dot_general x9, matrix products, body(): lax.dot_general(flat_x, shifted, (((0,), (0,)), ((), ())), preferred_elem...  25 us
    psum x1, blocking collectives, body(): lax.psum(lax.psum((jnp.sum(weights_pix), jnp.sum(weights_pix * cross)), '...  22.4 us
    another operation x1, local copies, waits for them, and re-layouts, body(): jnp.stack(parts_list, 1)  19 us
    psum x1, blocking collectives, body(): lax.psum((first_gradient_sum, second_gradient_sum, class_tile), 'rep')  18.3 us
    psum x1, blocking collectives, body(): column_sum = lax.psum(jnp.sum(yvals, 0), 'tile')  8.36 us
  transfers between devices with their start and end apart: 3, of which 3 were waited for; matrix products, arithmetic and copies ran while one was open for 21% of the time, Pallas kernels for 0%

profile of v1, /device:TPU:0, one launch (start us, length us, event | category | flops | bytes accessed | tf_op | source)
XLA Modules:
  0.0 390.1 jit_solution(4579871767185195462)
XLA Ops:
  8.7 8.4 %psum.84 = f32[256]{0:T(256)S(1)} all-reduce(f32[256]{0:T(256)S(1)} %convert_reduce_fusion), channel_id=1, replica_groups=mesh['rep'=8,'tile'=4] {'tile'}, use_global_device_ids=true, to_apply=%region_1.0 | all-reduce | flops 256 | bytes 2048 | tf_op jit(solution)/shard_map/psum | solution.py:42
  18.5 5.8 %psum.85 = f32[256]{0:T(256)S(1)} all-reduce(f32[256]{0:T(256)S(1)} %multiply_reduce_fusion.1), channel_id=1, replica_groups=mesh['rep'=8,'tile'=4] {'tile'}, use_global_device_ids=true, to_apply=%region_3.0 | all-reduce | flops 256 | bytes 2048 | tf_op jit(solution)/shard_map/psum | solution.py:44
  27.7 2.5 fusion.63
  30.9 6.4 %psum.86 = f32[]{:T(128)} all-reduce(f32[]{:T(128)} %get-tuple-element.31), channel_id=1, replica_groups=mesh['rep'=8,'tile'=4] {'tile'}, use_global_device_ids=true, to_apply=%region_6.0 | all-reduce | flops 1 | bytes 8 | tf_op jit(solution)/shard_map/psum | solution.py:58
  37.2 22.4 %psum.87 = f32[]{:T(128)} all-reduce(f32[]{:T(128)} %psum.86), channel_id=1, replica_groups=mesh['rep'=8,'tile'=4] {'rep'}, use_global_device_ids=true, to_apply=%region_7.0 | all-reduce | flops 1 | bytes 8 | tf_op jit(solution)/shard_map/psum | solution.py:57
  61.9 4.6 %fusion.61 = (f32[256]{0:T(256)S(1)}, f32[256]{0:T(256)S(1)}, f32[1728,256]{1,0:T(8,128)}) fusion(f32[256]{0:T(256)S(1)} %get-tuple-element.50, f32[256]{0:T(256)S(1)} %broadcast_multiply_fusion.1, bf16[2,12,72,256]{3,2,1,0:T(8,128)(2,1)} %param.9, f32[3,256]{1,0:T(4,128)S(1)} %copy-done, f32[1728,3]{0,1:T(4,128)S(1)} %get-tuple-element.52, ...), kind=kOutput, calls=%fused_computation.92 | convolution fusion | flops 20374336 | bytes 4474368 | tf_op jit(solution)/shard_map/dot_general | solution.py:65
  66.4 6.4 %all-reduce.2 = (f32[256]{0:T(256)S(1)}, f32[256]{0:T(256)S(1)}, f32[3,256]{1,0:T(4,128)S(1)}, f32[]{:T(128)}) all-reduce(f32[256]{0:T(256)S(1)} %get-tuple-element.25, f32[256]{0:T(256)S(1)} %get-tuple-element.24, f32[3,256]{1,0:T(4,128)S(1)} %fusion.16, f32[]{:T(128)} %get-tuple-element.40), channel_id=1, replica_groups=mesh['rep'=8,'tile'=4] {'tile'}, use_global_device_ids=true, to_apply=%region_13.0 | all-reduce | flops 1281 | bytes 10248 | tf_op jit(solution)/shard_map/psum | solution.py:67
  72.8 2.3 multiply_convert_fusion
  78.9 3.3 collective-permute-done.1
  82.2 1.8 fusion.5
  84.1 2.8 fusion.14
  87.0 2.8 fusion.13
  89.7 2.8 fusion.12
  92.5 2.8 fusion.11
  95.3 2.8 fusion.10
  98.1 2.8 fusion.9
  100.8 2.7 fusion.8
  103.6 2.8 fusion.7
  106.3 2.8 fusion.6
  109.1 19.0 %copy.18 = f32[1536,9,256]{2,1,0:T(8,128)} copy(f32[1536,9,256]{0,2,1:T(8,128)} %fusion.6) | data formatting | bytes 28311552 | tf_op jit(solution)/shard_map/stack | solution.py:115
  128.1 18.3 %all-reduce.1 = (f32[256]{0:T(256)}, f32[256]{0:T(256)}, f32[3,256]{1,0:T(4,128)}, f32[]{:T(128)}) all-reduce(f32[256]{0:T(256)S(1)} %get-tuple-element.36, f32[256]{0:T(256)S(1)} %get-tuple-element.37, f32[3,256]{1,0:T(4,128)S(1)} %get-tuple-element.38, f32[]{:T(128)} %get-tuple-element.39), channel_id=1, replica_groups=mesh['rep'=8,'tile'=4] {'rep'}, use_global_device_ids=true, to_apply=%region_15.16 | all-reduce | flops 1281 | bytes 10248 | tf_op jit(solution)/shard_map/psum | solution.py:75
  147.1 7.8 %fusion.33 = f32[1728,1536]{1,0:T(8,128)} fusion(bf16[1728,256]{1,0:T(8,128)(2,1)S(1)} %multiply_convert_fusion, bf16[9,1536,256]{2,1,0:T(8,128)(2,1)} %param.10), kind=kOutput, calls=%fused_computation.52 | convolution fusion | flops 1358954496 | bytes 12288000 | tf_op jit(solution)/shard_map/dot_general | solution.py:100
  155.5 8.2 %fusion.26 = f32[1728,1536]{1,0:T(8,128)} fusion(bf16[1728,256]{1,0:T(8,128)(2,1)S(1)} %bitcast.174, bf16[9,1536,256]{2,1,0:T(8,128)(2,1)} %param.10), kind=kOutput, calls=%fused_computation.45 | convolution fusion | flops 1358954496 | bytes 12288000 | tf_op jit(solution)/shard_map/dot_general | solution.py:100
  163.6 6.3 %fusion.29 = f32[1728,1536]{1,0:T(8,128)} fusion(bf16[1728,256]{1,0:T(8,128)(2,1)S(1)} %bitcast.173, bf16[9,1536,256]{2,1,0:T(8,128)(2,1)S(1)} %bitcast.167), kind=kOutput, calls=%fused_computation.48 | convolution fusion | flops 1358954496 | bytes 12288000 | tf_op jit(solution)/shard_map/dot_general | solution.py:100
  170.0 6.3 %fusion.31 = f32[1728,1536]{1,0:T(8,128)} fusion(bf16[1728,256]{1,0:T(8,128)(2,1)S(1)} %bitcast.172, bf16[9,1536,256]{2,1,0:T(8,128)(2,1)S(1)} %bitcast.167), kind=kOutput, calls=%fused_computation.50 | convolution fusion | flops 1358954496 | bytes 12288000 | tf_op jit(solution)/shard_map/dot_general | solution.py:100
  176.3 6.4 %fusion.35 = f32[1728,1536]{1,0:T(8,128)} fusion(bf16[1728,256]{1,0:T(8,128)(2,1)S(1)} %bitcast.171, bf16[9,1536,256]{2,1,0:T(8,128)(2,1)S(1)} %bitcast.167), kind=kOutput, calls=%fused_computation.54 | convolution fusion | flops 1358954496 | bytes 12288000 | tf_op jit(solution)/shard_map/dot_general | solution.py:100
  182.7 5.7 %fusion.37 = f32[1728,1536]{1,0:T(8,128)} fusion(bf16[1728,256]{1,0:T(8,128)(2,1)S(1)} %bitcast.170, bf16[9,1536,256]{2,1,0:T(8,128)(2,1)S(1)} %bitcast.167), kind=kOutput, calls=%fused_computation.56 | convolution fusion | flops 1358954496 | bytes 12288000 | tf_op jit(solution)/shard_map/dot_general | solution.py:100
  188.5 5.6 %fusion.41 = f32[1728,1536]{1,0:T(8,128)} fusion(bf16[1728,256]{1,0:T(8,128)(2,1)S(1)} %bitcast.169, bf16[9,1536,256]{2,1,0:T(8,128)(2,1)S(1)} %bitcast.167), kind=kOutput, calls=%fused_computation.60 | convolution fusion | flops 1358954496 | bytes 12288000 | tf_op jit(solution)/shard_map/dot_general | solution.py:100
  194.1 6.2 %fusion.39 = f32[1728,1536]{1,0:T(8,128)} fusion(bf16[1728,256]{1,0:T(8,128)(2,1)S(1)} %bitcast.164, bf16[9,1536,256]{2,1,0:T(8,128)(2,1)S(1)} %bitcast.167), kind=kOutput, calls=%fused_computation.58 | convolution fusion | flops 1358954496 | bytes 12288000 | tf_op jit(solution)/shard_map/dot_general | solution.py:100
  200.3 30.0 %add_convert_fusion = bf16[1728,1536]{1,0:T(8,128)(2,1)} fusion(f32[1728,1536]{1,0:T(8,128)} %fusion.26, f32[1728,1536]{1,0:T(8,128)} %fusion.29, f32[1728,1536]{1,0:T(8,128)} %fusion.31, f32[1728,1536]{1,0:T(8,128)} %fusion.33, f32[1728,1536]{1,0:T(8,128)} %fusion.35, f32[1728,1536]{1,0:T(8,128)} %fusion.37, f32[1728,1536]{1,0:T(8,128)} %fusion.41, ...), kind=kOutput, calls=%fused_computation.2 | convolution fusion | flops 1382842368 | bytes 91914240 | tf_op jit(solution)/shard_map/dot_general | solution.py:100
  230.3 149.6 %reduce-scatter.2.cloned.1.call-done = f32[48,9,256]{2,1,0:T(8,128)} async-done(((f32[1536,9,256]{2,1,0:T(8,128)}), f32[48,9,256]{2,1,0:T(8,128)}) %reduce-scatter.2.cloned.1.call-update) | async-done | bytes 442384 | tf_op jit(solution)/shard_map/reduce_scatter | solution.py:114
  379.9 2.2 copy.19
  (44 shorter events, 13.1 us)
Async XLA Ops:
  7.2 20.6 %copy-start = (f32[3,256]{1,0:T(4,128)S(1)}, f32[3,256]{1,0:T(4,128)}, u32[]{:S(2)}) copy-start(f32[3,256]{1,0:T(4,128)} %param.13) | copy-start | bytes 9220
  7.2 53.7 %copy-start.6 = (f32[256]{0:T(256)S(1)}, f32[256]{0:T(256)}, u32[]{:S(2)}) copy-start(f32[256]{0:T(256)} %param.11) | copy-start | bytes 3076
  7.2 53.7 %copy-start.7 = (f32[256]{0:T(256)S(1)}, f32[256]{0:T(256)}, u32[]{:S(2)}) copy-start(f32[256]{0:T(256)} %param.12) | copy-start | bytes 3076
  7.2 372.7 %reduce-scatter.2.cloned.1.call-start = ((), (), s32[]{:S(2)}) async-start(), calls=%async_computation.1 | async-start | bytes 25952256 | tf_op jit(solution)/shard_map/reduce_scatter | solution.py:114
  61.9 22.2 %slice-start = ((s8[5308416]{0:T(1024)(128)(4,1)}), s8[1114112]{0:T(1024)(128)(4,1)S(1)}, s32[]{:S(2)}) async-start(s8[5308416]{0:T(1024)(128)(4,1)} %bitcast.158), calls=%async_computation.2 | async-start | bytes 2228224
  72.8 11.3 %slice-start.1 = ((s8[5308416]{0:T(1024)(128)(4,1)}), s8[4194304]{0:T(1024)(128)(4,1)S(1)}, s32[]{:S(2)}) async-start(s8[5308416]{0:T(1024)(128)(4,1)} %bitcast.158), calls=%async_computation.3 | async-start | bytes 8388608
  75.2 3.8 collective-permute-start
  77.0 5.3 %collective-permute-start.1 = (bf16[2,12,72,256]{3,2,1,0:T(8,128)(2,1)S(1)}, bf16[2,12,72,256]{3,2,1,0:T(8,128)(2,1)S(1)}, u32[]{:S(2)}, u32[]{:S(2)}) collective-permute-start(bf16[2,12,72,256]{3,2,1,0:T(8,128)(2,1)S(1)} %bitcast.161), channel_id=1, source_target_pairs={{1,0},{2,1},{3,2},{5,4},{6,5},{7,6},{9,8},{10,9},{11,10},{13,12},{... | collective-permute-start | bytes 2654216 | tf_op jit(solution)/shard_map/ppermute | solution.py:20
  78.9 24.6 %copy-start.4 = (bf16[2,12,72,256]{3,2,1,0:T(8,128)(2,1)}, bf16[2,12,72,256]{3,2,1,0:T(8,128)(2,1)S(1)}, u32[]{:S(2)}) copy-start(bf16[2,12,72,256]{3,2,1,0:T(8,128)(2,1)S(1)} %collective-permute-done) | copy-start | bytes 2654212
  84.1 22.2 %copy-start.2 = (bf16[2,36,96,256]{3,2,1,0:T(8,128)(2,1)}, bf16[2,36,96,256]{3,2,1,0:T(8,128)(2,1)S(1)}, u32[]{:S(2)}) copy-start(bf16[2,36,96,256]{3,2,1,0:T(8,128)(2,1)S(1)} %fusion.5) | copy-start | bytes 10616836
  147.1 7.8 %copy-start.3 = (bf16[2,36,96,256]{3,2,1,0:T(8,128)(2,1)S(1)}, bf16[2,36,96,256]{3,2,1,0:T(8,128)(2,1)}, u32[]{:S(2)}) copy-start(bf16[2,36,96,256]{3,2,1,0:T(8,128)(2,1)} %copy-done.2) | copy-start | bytes 10616836
  154.8 8.8 %slice-start.2 = ((s8[7077888]{0:T(1024)(128)(4,1)}), s8[2883584]{0:T(1024)(128)(4,1)S(1)}, s32[]{:S(2)}) async-start(s8[7077888]{0:T(1024)(128)(4,1)} %bitcast.166), calls=%async_computation.4 | async-start | bytes 5767168
  155.4 8.2 %slice-start.3 = ((s8[7077888]{0:T(1024)(128)(4,1)}), s8[4194304]{0:T(1024)(128)(4,1)S(1)}, s32[]{:S(2)}) async-start(s8[7077888]{0:T(1024)(128)(4,1)} %bitcast.166), calls=%async_computation.5 | async-start | bytes 8388608
  194.1 6.2 %copy-start.5 = (bf16[2,12,72,256]{3,2,1,0:T(8,128)(2,1)S(1)}, bf16[2,12,72,256]{3,2,1,0:T(8,128)(2,1)}, u32[]{:S(2)}) copy-start(bf16[2,12,72,256]{3,2,1,0:T(8,128)(2,1)} %copy-done.4) | copy-start | bytes 2654212
  200.3 181.8 %copy-start.1 = (f32[3,256]{1,0:T(4,128)S(1)}, f32[3,256]{1,0:T(4,128)}, u32[]{:S(2)}) copy-start(f32[3,256]{1,0:T(4,128)} %param.13) | copy-start | bytes 9220
Sparse Core Ops, SparseCore 0:
  128.2 251.6 reduce-scatter.1
